TPU v7x, 256 devices: a whole 4x4x8 slice. The times are simulated.
256 devices in a mesh: row: 8 (over z_lo, y), col: 32 (over z_hi, x, core).
Axes of the slice: x: 4, y: 4, z: 8 (z_hi: 4, z_lo: 2; z = z_hi * 2 + z_lo), core: 2. Of those that a mesh axis runs over, the one named last changes fastest.
Arguments:
- strip: float32 [12, 2048, 2, 1024], P(None, 'col', None, 'row'), may hold values from -6 to 6
- lower: float32 [12, 2048, 2, 1024], P(None, 'col', None, 'row'), may hold values from -1.6 to 1.6, as said below
Outputs:
- reduced: float32 [12, 2048, 2, 1024], P(None, 'col', None, 'row')
Inputs may be any that keep to these rules, and one draw needn't show every extreme that they name: `lower`: in the first 2048 rows the diagonal lies between 0.8 and 1.6 and entries above it are zero.
All inputs are finite; a program needn't handle non-finite values.
Results may differ from a plain program's by a relative error of at most 0.00013.
Values sent between devices are 32-bit elements; how exact they have to be, the bound alone decides.
No kernel may reach another device: no remote copies, remote signals or barrier semaphores. Data moves between devices by JAX's collectives and lax.ppermute only.
A program may use at most 64 MiB of HBM per device.

v0:
```python
import jax
import jax.numpy as jnp
from jax import lax
from jax.sharding import PartitionSpec as P

highest = lax.Precision.HIGHEST


def times_rows(coeff, right_side):
    return jnp.dot(coeff, right_side, precision=highest, preferred_element_type=jnp.float32)


def times_rows_turned(coeff, right_turned):
    return lax.dot_general(
        coeff,
        right_turned,
        (((1,), (1,)), ((), ())),
        precision=highest,
        preferred_element_type=jnp.float32,
    )


def local(strip, lower):
    rounds = strip.shape[0]
    strip_width = strip.shape[1]
    row_run = strip.shape[3]
    row_count = lax.axis_size("row")
    col_count = lax.axis_size("col")
    block_size = row_run * row_count
    cols_here = rounds * strip_width
    trail_count = cols_here - strip_width
    share = block_size // col_count
    local_strip = strip.reshape(cols_here, 2, row_run)
    left_part = local_strip[:, 0, :]
    right_part = local_strip[:, 1, :]
    gathered = lax.all_gather(lower[0], "col", axis=0, tiled=True)
    first_cols = gathered[:block_size, 0, :]
    cross_cols = gathered[block_size:, 0, :]
    second_cols = gathered[block_size:, 1, :]
    col_position = lax.axis_index("col")
    start = col_position * share
    top_rows = lax.dynamic_slice_in_dim(gathered, start, share, 0)
    bottom_rows = lax.dynamic_slice_in_dim(gathered, block_size + start, share, 0)
    picked = jnp.concatenate([top_rows, bottom_rows], axis=0)
    picked_rows = lax.all_gather(picked, "row", axis=2, tiled=True)
    first_rows = picked_rows[:share, 0, :]
    cross_rows = picked_rows[share:, 0, :]
    second_rows = picked_rows[share:, 1, :]
    upper_half = lax.psum_scatter(
        times_rows_turned(first_cols, left_part), "row", scatter_dimension=0, tiled=True
    )
    carried = lax.psum_scatter(
        times_rows(cross_cols, upper_half), "row", scatter_dimension=0, tiled=True
    )
    remainder = right_part.T - carried
    lower_half = lax.psum_scatter(
        times_rows(second_cols, remainder), "row", scatter_dimension=0, tiled=True
    )
    solved = jnp.stack([upper_half.T, lower_half.T], axis=1)
    lead_rows = solved[:strip_width]
    tail_rows = solved[strip_width:].reshape(trail_count, 2 * row_run)
    lead_all = lax.all_gather(lead_rows, "col", axis=0, tiled=True)
    lead_all = lead_all.reshape(2 * block_size, 2 * row_run)
    first_piece = times_rows(first_rows, lead_all[:block_size])
    first_block = lax.all_gather(first_piece, "col", axis=0, tiled=True)
    lead_second = lax.dynamic_slice_in_dim(lead_all, block_size + start, share, 0)
    diff_piece = lead_second - times_rows(cross_rows, first_block)
    diff_block = lax.all_gather(diff_piece, "col", axis=0, tiled=True)
    second_piece = times_rows(second_rows, diff_block)
    second_block = lax.all_gather(second_piece, "col", axis=0, tiled=True)
    everything = jnp.concatenate([first_block, second_block], axis=0)
    solved_lead = lax.dynamic_slice_in_dim(everything, col_position * strip_width, strip_width, 0)
    left_rows = lower[1:].reshape(trail_count, 2 * row_run)
    grouped = everything.reshape(2, row_count, row_run, 2 * row_run).transpose(1, 0, 2, 3)
    swapped = lax.all_to_all(grouped, "row", split_axis=0, concat_axis=0, tiled=True)
    turned_block = swapped.reshape(row_count, 2, row_run, 2, row_run).transpose(0, 3, 4, 1, 2)
    turned_block = turned_block.reshape(row_count * 2 * row_run, 2 * row_run)
    summed = lax.psum_scatter(
        times_rows_turned(turned_block, left_rows), "row", scatter_dimension=0, tiled=True
    )
    update = summed.T
    reduced = jnp.concatenate([solved_lead, tail_rows - update], axis=0)
    return reduced.reshape(rounds, strip_width, 2, row_run)


def solution(mesh):
    in_specs = (P(None, "col", None, "row"), P(None, "col", None, "row"))
    out_specs = P(None, "col", None, "row")
    return jax.shard_map(local, mesh=mesh, in_specs=in_specs, out_specs=out_specs, check_vma=False)
```

profile of v0, /device:TPU:1, one launch (start us, length us, event | category | flops | bytes accessed | tf_op | source)
XLA Modules:
  0.0 562.7 jit_solution(11136738738206330280)
XLA Ops:
  6.5 1.5 slice_bitcast_fusion.3
  8.1 1.2 copy.9
  9.3 59.5 %all-gather.15.cloned.1.call-done = f32[1,2048,2,128]{3,2,0,1:T(2,128)} async-done(((f32[1,64,2,128]{3,2,0,1:T(2,128)}), f32[1,2048,2,128]{3,2,0,1:T(2,128)}) %all-gather.15.cloned.1.call-update) | async-done | bytes 2097168 | tf_op jit(solution)/shard_map/all_gather | solution.py:36
  68.8 3.2 fusion.18
  72.1 4.3 fusion.10
  76.4 41.6 %reduce-scatter.5.cloned.1.call-done = f32[128,768]{1,0:T(8,128)} async-done(((f32[1024,768]{1,0:T(8,128)}), f32[128,768]{1,0:T(8,128)}) %reduce-scatter.5.cloned.1.call-update) | async-done | bytes 393232 | tf_op jit(solution)/shard_map/reduce_scatter | solution.py:49
  118.0 5.3 convolution_bitcast_fusion.1
  123.4 48.2 %reduce-scatter.7.cloned.1.call-done = f32[128,768]{0,1:T(8,128)} async-done(((f32[1024,768]{0,1:T(8,128)}), f32[128,768]{0,1:T(8,128)}) %reduce-scatter.7.cloned.1.call-update) | async-done | bytes 393232 | tf_op jit(solution)/shard_map/reduce_scatter | solution.py:52
  171.6 5.3 convolution_bitcast_fusion
  177.0 48.3 %reduce-scatter.9.cloned.1.call-done = f32[128,768]{1,0:T(8,128)} async-done(((f32[1024,768]{1,0:T(8,128)}), f32[128,768]{1,0:T(8,128)}) %reduce-scatter.9.cloned.1.call-update) | async-done | bytes 393232 | tf_op jit(solution)/shard_map/reduce_scatter | solution.py:56
  227.7 16.4 %all_gather.19 = f32[64,2,1024]{2,1,0:T(2,128)S(1)} all-gather(f32[64,2,128]{2,1,0:T(2,128)S(1)} %pad_maximum_fusion.3), channel_id=1, replica_groups=mesh['row'=8,'col'=32] {'row'}, dimensions={2}, use_global_device_ids=true | all-gather | bytes 589824 | tf_op jit(solution)/shard_map/all_gather | solution.py:45
  244.1 1.0 fusion.19
  245.1 41.1 %all-gather.7.cloned.1.call-done = f32[2048,2,128]{2,1,0:T(2,128)} async-done(((f32[64,2,128]{2,1,0:T(2,128)}), f32[2048,2,128]{2,1,0:T(2,128)}) %all-gather.7.cloned.1.call-update) | async-done | bytes 2097168 | tf_op jit(solution)/shard_map/all_gather | solution.py:62
  286.2 1.2 slice-done
  287.4 2.1 fusion.3
  289.8 1.5 copy.51
  291.3 47.4 %all-gather.9.cloned.1.call-done = f32[1024,256]{1,0:T(8,128)} async-done(((f32[32,256]{1,0:T(8,128)}), f32[1024,256]{1,0:T(8,128)}) %all-gather.9.cloned.1.call-update) | async-done | bytes 1048592 | tf_op jit(solution)/shard_map/all_gather | solution.py:65
  338.7 2.5 convolution_subtract_fusion
  341.3 49.6 %all-gather.11.cloned.1.call-done = f32[1024,256]{1,0:T(8,128)} async-done(((f32[32,256]{1,0:T(8,128)}), f32[1024,256]{1,0:T(8,128)}) %all-gather.11.cloned.1.call-update) | async-done | bytes 1048592 | tf_op jit(solution)/shard_map/all_gather | solution.py:68
  390.9 2.4 fusion.13
  393.4 49.5 %all-gather.13.cloned.1.call-done = f32[1024,256]{1,0:T(8,128)} async-done(((f32[32,256]{1,0:T(8,128)}), f32[1024,256]{1,0:T(8,128)}) %all-gather.13.cloned.1.call-update) | async-done | bytes 1048592 | tf_op jit(solution)/shard_map/all_gather | solution.py:70
  443.0 1.3 constant_dynamic-update-slice_fusion
  444.3 1.7 copy.52
  446.2 4.3 all-to-all-start
  450.7 26.2 %all-to-all-done = f32[8,2,128,256]{3,2,1,0:T(8,128)} async-done(((f32[8,2,128,256]{3,2,1,0:T(8,128)}), f32[8,2,128,256]{3,2,1,0:T(8,128)}, u32[]{:S(2)}, u32[]{:S(2)}) %all-to-all-start) | async-done | bytes 2097184 | tf_op jit(solution)/shard_map/all_to_all | solution.py:75
  476.8 2.8 copy.16
  479.7 6.7 %fusion = f32[2048,704]{0,1:T(8,128)} fusion(f32[256,8,2,128]{3,2,1,0:T(2,128)S(1)} %bitcast.74, f32[88,8,2,128]{3,2,1,0:T(2,128)S(1)} %bitcast.83), kind=kOutput, calls=%fused_computation | convolution fusion | flops 4429185024 | bytes 8585216 | tf_op jit(solution)/shard_map/dot_general | solution.py:14
  486.4 1.0 copy-done.4
  487.9 0.9 constant_dynamic-slice_fusion
  488.7 64.9 %reduce-scatter.11.cloned.1.call-done = f32[256,704]{0,1:T(8,128)} async-done(((f32[2048,704]{0,1:T(8,128)}), f32[256,704]{0,1:T(8,128)}) %reduce-scatter.11.cloned.1.call-update) | async-done | bytes 720912 | tf_op jit(solution)/shard_map/reduce_scatter | solution.py:78
  553.6 1.2 bitcast_subtract_fusion
  554.9 1.3 reshape.32
  (42 shorter events, 4.0 us)
Async XLA Ops:
  6.5 62.3 %all-gather.15.cloned.1.call-start = ((), (), s32[]{:S(2)}) async-start(), calls=%async_computation.13 | async-start | bytes 2162688 | tf_op jit(solution)/shard_map/all_gather | solution.py:36
  8.0 110.0 %reduce-scatter.5.cloned.1.call-start = ((), (), s32[]{:S(2)}) async-start(), calls=%async_computation.5 | async-start | bytes 3538944 | tf_op jit(solution)/shard_map/reduce_scatter | solution.py:49
  76.4 95.3 %reduce-scatter.7.cloned.1.call-start = ((), (), s32[]{:S(2)}) async-start(), calls=%async_computation.6 | async-start | bytes 3538944 | tf_op jit(solution)/shard_map/reduce_scatter | solution.py:52
  123.3 101.9 %reduce-scatter.9.cloned.1.call-start = ((), (), s32[]{:S(2)}) async-start(), calls=%async_computation.7 | async-start | bytes 3538944 | tf_op jit(solution)/shard_map/reduce_scatter | solution.py:56
  176.9 48.4 %copy-start.3 = (f32[128,768]{1,0:T(8,128)S(1)}, f32[128,768]{1,0:T(8,128)}, u32[]{:S(2)}) copy-start(f32[128,768]{1,0:T(8,128)} %reduce-scatter.5.cloned.1.call-done) | copy-start | bytes 1179652
  176.9 109.3 %all-gather.7.cloned.1.call-start = ((), (), s32[]{:S(2)}) async-start(), calls=%async_computation.8 | async-start | bytes 2162688 | tf_op jit(solution)/shard_map/all_gather | solution.py:62
  226.8 111.9 %all-gather.9.cloned.1.call-start = ((), (), s32[]{:S(2)}) async-start(), calls=%async_computation.9 | async-start | bytes 1081344 | tf_op jit(solution)/shard_map/all_gather | solution.py:65
  286.2 1.2 slice-start
  286.2 3.6 copy-start.1
  289.5 101.4 %all-gather.11.cloned.1.call-start = ((), (), s32[]{:S(2)}) async-start(), calls=%async_computation.10 | async-start | bytes 1081344 | tf_op jit(solution)/shard_map/all_gather | solution.py:68
  289.8 49.0 %copy-start.6 = (f32[32,1,1024]{2,1,0:T(1,128)S(1)}, f32[32,1,1024]{2,1,0:T(1,128)}, u32[]{:S(2)}) copy-start(f32[32,1,1024]{2,1,0:T(1,128)} %get-tuple-element.11) | copy-start | bytes 393220
  289.8 101.1 %copy-start.5 = (f32[32,1,1024]{2,1,0:T(1,128)S(1)}, f32[32,1,1024]{2,1,0:T(1,128)}, u32[]{:S(2)}) copy-start(f32[32,1,1024]{2,1,0:T(1,128)} %get-tuple-element.10) | copy-start | bytes 393220
  338.7 54.6 %copy-start.2 = (f32[1024,256]{1,0:T(8,128)S(1)}, f32[1024,256]{1,0:T(8,128)}, u32[]{:S(2)}) copy-start(f32[1024,256]{1,0:T(8,128)} %all-gather.9.cloned.1.call-done) | copy-start | bytes 3145732
  341.3 101.7 %all-gather.13.cloned.1.call-start = ((), (), s32[]{:S(2)}) async-start(), calls=%async_computation.11 | async-start | bytes 1081344 | tf_op jit(solution)/shard_map/all_gather | solution.py:70
  444.3 2.0 copy-start
  446.2 30.6 %all-to-all-start = ((f32[8,2,128,256]{3,2,1,0:T(8,128)}), f32[8,2,128,256]{3,2,1,0:T(8,128)}, u32[]{:S(2)}, u32[]{:S(2)}) async-start(f32[8,2,128,256]{3,2,1,0:T(8,128)} %bitcast.73), calls=%async_computation.3 | async-start | bytes 4194304 | tf_op jit(solution)/shard_map/all_to_all | solution.py:75
  450.6 103.0 %reduce-scatter.11.cloned.1.call-start = ((), (), s32[]{:S(2)}) async-start(), calls=%async_computation.12 | async-start | bytes 6488064 | tf_op jit(solution)/shard_map/reduce_scatter | solution.py:78
  450.6 29.0 %slice-start.1 = ((f32[12,64,2,128]{3,2,1,0:T(2,128)}), f32[11,64,2,128]{3,2,1,0:T(2,128)S(1)}, s32[]{:S(2)}) async-start(f32[12,64,2,128]{3,2,1,0:T(2,128)} %param.3), calls=%async_computation.15 | async-start | bytes 1441792 | tf_op jit(solution)/shard_map/slice | solution.py:73
  486.3 1.0 copy-start.4
Sparse Core Ops, SparseCore 0:
  9.9 58.8 all-gather.14
  76.5 41.5 reduce-scatter.4
  123.5 48.1 reduce-scatter.6
  177.0 48.1 reduce-scatter.8
  227.6 58.4 all-gather.6
  289.6 49.0 all-gather.8
  341.4 49.4 all-gather.10
  393.5 49.4 all-gather.12
  486.5 67.0 reduce-scatter.10
where the time goes:
time: 563 us
  waiting for transfers between devices  476 us (85%)
  matrix products  28.5 us (5%)
  local copies, waits for them, and re-layouts  20.7 us (4%)
  blocking collectives  16.4 us (3%)
  between operations  13.3 us (2%)
    reduce_scatter x1, waiting for transfers between devices, local(): lax.psum_scatter(times_rows_turned(turned_block, left_rows), 'row', scatt...  64.9 us
    all_gather x1, waiting for transfers between devices, local(): gathered = lax.all_gather(lower[0], 'col', axis=0, tiled=True)  59.5 us
    all_gather x1, waiting for transfers between devices, local(): diff_block = lax.all_gather(diff_piece, 'col', axis=0, tiled=True)  49.6 us
    all_gather x1, waiting for transfers between devices, local(): second_block = lax.all_gather(second_piece, 'col', axis=0, tiled=True)  49.5 us
    reduce_scatter x1, waiting for transfers between devices, local(): lax.psum_scatter(times_rows(second_cols, remainder), 'row', scatter_dimen...  48.3 us
    reduce_scatter x1, waiting for transfers between devices, local(): lax.psum_scatter(times_rows(cross_cols, upper_half), 'row', scatter_dimen...  48.2 us
    all_gather x1, waiting for transfers between devices, local(): first_block = lax.all_gather(first_piece, 'col', axis=0, tiled=True)  47.4 us
    reduce_scatter x1, waiting for transfers between devices, local(): lax.psum_scatter(times_rows_turned(first_cols, left_part), 'row', scatter...  41.6 us
  transfers between devices with their start and end apart: 10, of which 10 were waited for; matrix products, arithmetic and copies ran while one was open for 1% of the time, Pallas kernels for 0%

commit v1 on v0

--- a/solution.py
+++ b/solution.py
@@ -59,7 +59,9 @@
     solved = jnp.stack([upper_half.T, lower_half.T], axis=1)
     lead_rows = solved[:strip_width]
     tail_rows = solved[strip_width:].reshape(trail_count, 2 * row_run)
-    lead_all = lax.all_gather(lead_rows, "col", axis=0, tiled=True)
+    lead_all = jnp.concatenate(
+        lax.all_to_all(jnp.stack([lead_rows] * lax.axis_size("col")), "col", 0, 0), axis=0
+    )
     lead_all = lead_all.reshape(2 * block_size, 2 * row_run)
     first_piece = times_rows(first_rows, lead_all[:block_size])
     first_block = lax.all_gather(first_piece, "col", axis=0, tiled=True)

time: 563 us -> 582 us (1.034)
  blocking collectives: 16.4 us -> 59 us
  waiting for transfers between devices: 476 us -> 440 us
  starting transfers between devices: 4.86 us -> 17.6 us
    all_gather x1, blocking collectives: 16.4 us -> 59 us  [local(): picked_rows = lax.all_gather(picked, 'row', axis=2, tiled=True)]
    all_gather x1 -> x0, waiting for transfers between devices: 41.1 us -> none  [local(): lead_all = lax.all_gather(lead_rows, 'col', axis=0, tiled=True)]
    all_to_all x0 -> x1, starting transfers between devices: none -> 13 us  [local(): lax.all_to_all(jnp.stack([lead_rows] * lax.axis_size('col')), 'col', 0, 0)]
  transfers between devices with their start and end apart: 10 -> 10, of which waited for: 10 -> 9; matrix products, arithmetic and copies ran while one was open for 1% -> 1% of each run, Pallas kernels for 0% -> 0%
where the time goes in v1:
time: 582 us; the launch traced here: 581 us
  waiting for transfers between devices  440 us (76%)
  blocking collectives  59 us (10%)
  matrix products  27.7 us (5%)
  local copies, waits for them, and re-layouts  21.1 us (4%)
  starting transfers between devices  17.6 us (3%)
  between operations  13.6 us (2%)
    reduce_scatter x1, waiting for transfers between devices, local(): lax.psum_scatter(times_rows_turned(turned_block, left_rows), 'row', scatt...  64.9 us
    all_gather x1, waiting for transfers between devices, local(): gathered = lax.all_gather(lower[0], 'col', axis=0, tiled=True)  59.5 us
    all_gather x1, blocking collectives, local(): picked_rows = lax.all_gather(picked, 'row', axis=2, tiled=True)  59 us
    all_gather x1, waiting for transfers between devices, local(): first_block = lax.all_gather(first_piece, 'col', axis=0, tiled=True)  51.9 us
    all_gather x1, waiting for transfers between devices, local(): diff_block = lax.all_gather(diff_piece, 'col', axis=0, tiled=True)  49.6 us
    all_gather x1, waiting for transfers between devices, local(): second_block = lax.all_gather(second_piece, 'col', axis=0, tiled=True)  49.5 us
    reduce_scatter x1, waiting for transfers between devices, local(): lax.psum_scatter(times_rows(second_cols, remainder), 'row', scatter_dimen...  48.5 us
    reduce_scatter x1, waiting for transfers between devices, local(): lax.psum_scatter(times_rows(cross_cols, upper_half), 'row', scatter_dimen...  48.4 us
  transfers between devices with their start and end apart: 10, of which 9 were waited for; matrix products, arithmetic and copies ran while one was open for 1% of the time, Pallas kernels for 0%

profile of v1, /device:TPU:1, one launch (start us, length us, event | category | flops | bytes accessed | tf_op | source)
XLA Modules:
  0.0 581.4 jit_solution(7855718678855229006)
XLA Ops:
  6.5 1.5 slice_bitcast_fusion.3
  8.1 1.2 copy.11
  9.3 59.5 %all-gather.12.cloned.1.call-done = f32[1,2048,2,128]{3,2,0,1:T(2,128)} async-done(((f32[1,64,2,128]{3,2,0,1:T(2,128)}), f32[1,2048,2,128]{3,2,0,1:T(2,128)}) %all-gather.12.cloned.1.call-update) | async-done | bytes 2097168 | tf_op jit(solution)/shard_map/all_gather | solution.py:36
  68.8 3.3 fusion.18
  72.1 4.2 fusion.10
  76.4 41.4 %reduce-scatter.5.cloned.1.call-done = f32[128,768]{1,0:T(8,128)} async-done(((f32[1024,768]{1,0:T(8,128)}), f32[128,768]{1,0:T(8,128)}) %reduce-scatter.5.cloned.1.call-update) | async-done | bytes 393232 | tf_op jit(solution)/shard_map/reduce_scatter | solution.py:49
  117.9 5.3 convolution_bitcast_fusion.1
  123.2 48.4 %reduce-scatter.7.cloned.1.call-done = f32[128,768]{0,1:T(8,128)} async-done(((f32[1024,768]{0,1:T(8,128)}), f32[128,768]{0,1:T(8,128)}) %reduce-scatter.7.cloned.1.call-update) | async-done | bytes 393232 | tf_op jit(solution)/shard_map/reduce_scatter | solution.py:52
  171.6 5.3 convolution_bitcast_fusion
  176.9 48.5 %reduce-scatter.9.cloned.1.call-done = f32[128,768]{1,0:T(8,128)} async-done(((f32[1024,768]{1,0:T(8,128)}), f32[128,768]{1,0:T(8,128)}) %reduce-scatter.9.cloned.1.call-update) | async-done | bytes 393232 | tf_op jit(solution)/shard_map/reduce_scatter | solution.py:56
  226.4 2.3 stack.11
  228.6 13.0 %all-to-all-start = ((f32[32,64,2,128]{3,2,1,0:T(2,128)}), f32[32,64,2,128]{3,2,1,0:T(2,128)S(1)}, u32[]{:S(2)}, u32[]{:S(2)}) async-start(f32[32,64,2,128]{3,2,1,0:T(2,128)} %stack.11), calls=%async_computation.3 | async-start | bytes 4194304 | tf_op jit(solution)/shard_map/all_to_all | solution.py:63
  242.5 59.0 %all_gather.16 = f32[64,2,1024]{2,1,0:T(2,128)S(1)} all-gather(f32[64,2,128]{2,1,0:T(2,128)S(1)} %pad_maximum_fusion.3), channel_id=1, replica_groups=mesh['row'=8,'col'=32] {'row'}, dimensions={2}, use_global_device_ids=true | all-gather | bytes 589824 | tf_op jit(solution)/shard_map/all_gather | solution.py:45
  301.5 1.0 fusion.19
  302.5 1.2 fusion.3
  303.8 1.5 copy.53
  305.3 51.9 %all-gather.6.cloned.1.call-done = f32[1024,256]{1,0:T(8,128)} async-done(((f32[32,256]{1,0:T(8,128)}), f32[1024,256]{1,0:T(8,128)}) %all-gather.6.cloned.1.call-update) | async-done | bytes 1048592 | tf_op jit(solution)/shard_map/all_gather | solution.py:67
  357.2 2.5 convolution_subtract_fusion
  359.7 49.6 %all-gather.8.cloned.1.call-done = f32[1024,256]{1,0:T(8,128)} async-done(((f32[32,256]{1,0:T(8,128)}), f32[1024,256]{1,0:T(8,128)}) %all-gather.8.cloned.1.call-update) | async-done | bytes 1048592 | tf_op jit(solution)/shard_map/all_gather | solution.py:70
  409.3 2.5 fusion.13
  411.9 49.5 %all-gather.10.cloned.1.call-done = f32[1024,256]{1,0:T(8,128)} async-done(((f32[32,256]{1,0:T(8,128)}), f32[1024,256]{1,0:T(8,128)}) %all-gather.10.cloned.1.call-update) | async-done | bytes 1048592 | tf_op jit(solution)/shard_map/all_gather | solution.py:72
  461.5 1.3 constant_dynamic-update-slice_fusion
  462.8 1.7 copy.54
  464.7 4.3 all-to-all-start.1
  469.1 26.2 %all-to-all-done.1 = f32[8,2,128,256]{3,2,1,0:T(8,128)} async-done(((f32[8,2,128,256]{3,2,1,0:T(8,128)}), f32[8,2,128,256]{3,2,1,0:T(8,128)}, u32[]{:S(2)}, u32[]{:S(2)}) %all-to-all-start.1) | async-done | bytes 2097184 | tf_op jit(solution)/shard_map/all_to_all | solution.py:77
  495.3 2.8 copy.18
  498.2 6.7 %fusion = f32[2048,704]{0,1:T(8,128)} fusion(f32[256,8,2,128]{3,2,1,0:T(2,128)S(1)} %bitcast.76, f32[88,8,2,128]{3,2,1,0:T(2,128)S(1)} %bitcast.85), kind=kOutput, calls=%fused_computation | convolution fusion | flops 4429185024 | bytes 8585216 | tf_op jit(solution)/shard_map/dot_general | solution.py:14
  504.8 1.0 copy-done.3
  506.3 0.9 constant_dynamic-slice_fusion
  507.2 64.9 %reduce-scatter.11.cloned.1.call-done = f32[256,704]{0,1:T(8,128)} async-done(((f32[2048,704]{0,1:T(8,128)}), f32[256,704]{0,1:T(8,128)}) %reduce-scatter.11.cloned.1.call-update) | async-done | bytes 720912 | tf_op jit(solution)/shard_map/reduce_scatter | solution.py:80
  572.1 1.2 bitcast_subtract_fusion
  573.3 1.3 reshape.30
  (35 shorter events, 3.2 us)
Async XLA Ops:
  6.5 62.3 %all-gather.12.cloned.1.call-start = ((), (), s32[]{:S(2)}) async-start(), calls=%async_computation.13 | async-start | bytes 2162688 | tf_op jit(solution)/shard_map/all_gather | solution.py:36
  8.0 109.8 %reduce-scatter.5.cloned.1.call-start = ((), (), s32[]{:S(2)}) async-start(), calls=%async_computation.6 | async-start | bytes 3538944 | tf_op jit(solution)/shard_map/reduce_scatter | solution.py:49
  76.4 95.2 %reduce-scatter.7.cloned.1.call-start = ((), (), s32[]{:S(2)}) async-start(), calls=%async_computation.7 | async-start | bytes 3538944 | tf_op jit(solution)/shard_map/reduce_scatter | solution.py:52
  123.2 102.2 %reduce-scatter.9.cloned.1.call-start = ((), (), s32[]{:S(2)}) async-start(), calls=%async_computation.8 | async-start | bytes 3538944 | tf_op jit(solution)/shard_map/reduce_scatter | solution.py:56
  176.9 48.6 %copy-start.2 = (f32[128,768]{1,0:T(8,128)S(1)}, f32[128,768]{1,0:T(8,128)}, u32[]{:S(2)}) copy-start(f32[128,768]{1,0:T(8,128)} %reduce-scatter.5.cloned.1.call-done) | copy-start | bytes 1179652
  228.6 73.8 %all-to-all-start = ((f32[32,64,2,128]{3,2,1,0:T(2,128)}), f32[32,64,2,128]{3,2,1,0:T(2,128)S(1)}, u32[]{:S(2)}, u32[]{:S(2)}) async-start(f32[32,64,2,128]{3,2,1,0:T(2,128)} %stack.11), calls=%async_computation.3 | async-start | bytes 4194304 | tf_op jit(solution)/shard_map/all_to_all | solution.py:63
  241.6 115.5 %all-gather.6.cloned.1.call-start = ((), (), s32[]{:S(2)}) async-start(), calls=%async_computation.9 | async-start | bytes 1081344 | tf_op jit(solution)/shard_map/all_gather | solution.py:67
  303.8 105.6 %all-gather.8.cloned.1.call-start = ((), (), s32[]{:S(2)}) async-start(), calls=%async_computation.10 | async-start | bytes 1081344 | tf_op jit(solution)/shard_map/all_gather | solution.py:70
  357.1 54.7 %copy-start.1 = (f32[1024,256]{1,0:T(8,128)S(1)}, f32[1024,256]{1,0:T(8,128)}, u32[]{:S(2)}) copy-start(f32[1024,256]{1,0:T(8,128)} %all-gather.6.cloned.1.call-done) | copy-start | bytes 3145732
  359.7 101.8 %all-gather.10.cloned.1.call-start = ((), (), s32[]{:S(2)}) async-start(), calls=%async_computation.11 | async-start | bytes 1081344 | tf_op jit(solution)/shard_map/all_gather | solution.py:72
  462.8 1.9 copy-start
  464.7 30.6 %all-to-all-start.1 = ((f32[8,2,128,256]{3,2,1,0:T(8,128)}), f32[8,2,128,256]{3,2,1,0:T(8,128)}, u32[]{:S(2)}, u32[]{:S(2)}) async-start(f32[8,2,128,256]{3,2,1,0:T(8,128)} %bitcast.75), calls=%async_computation.4 | async-start | bytes 4194304 | tf_op jit(solution)/shard_map/all_to_all | solution.py:77
  469.1 103.0 %reduce-scatter.11.cloned.1.call-start = ((), (), s32[]{:S(2)}) async-start(), calls=%async_computation.12 | async-start | bytes 6488064 | tf_op jit(solution)/shard_map/reduce_scatter | solution.py:80
  469.1 29.0 %slice-start = ((f32[12,64,2,128]{3,2,1,0:T(2,128)}), f32[11,64,2,128]{3,2,1,0:T(2,128)S(1)}, s32[]{:S(2)}) async-start(f32[12,64,2,128]{3,2,1,0:T(2,128)} %param.3), calls=%async_computation.14 | async-start | bytes 1441792 | tf_op jit(solution)/shard_map/slice | solution.py:75
  504.8 1.0 copy-start.3
Sparse Core Ops, SparseCore 0:
  9.9 58.8 all-gather.11
  76.5 41.3 reduce-scatter.4
  123.3 48.2 reduce-scatter.6
  177.0 48.3 reduce-scatter.8
  303.9 53.2 all-gather.5
  359.8 49.4 all-gather.7
  412.0 49.4 all-gather.9
  505.0 67.0 reduce-scatter.10
